TPU v7x, 32 devices: a whole 2x2x4 slice. The times are simulated.
32 devices in a mesh: row: 8 (over z, y), col: 4 (over x, core).
Axes of the slice: x: 2, y: 2, z: 4, core: 2. Of those that a mesh axis runs over, the one named last changes fastest.
Arguments:
- gram: float32 [16384, 16384], P('row', 'col'), may hold values from -1 to 17, as said below
Outputs:
- factored: float32 [16384, 16384], P('row', 'col')
Inputs may be any that keep to these rules, and one draw needn't show every extreme that they name: gram holds a symmetric positive definite matrix in the block-cyclic order of the steps.
All inputs are finite; a program needn't handle non-finite values.
Results may differ from a plain program's by a relative error of at most 0.0001.
Values sent between devices are 32-bit elements; how exact they have to be, the bound alone decides.
No kernel may reach another device: no remote copies, remote signals or barrier semaphores. Data moves between devices by JAX's collectives and lax.ppermute only.
A program may use at most 192 MiB of HBM per device.

v0:
```python
import jax
import jax.numpy as jnp
from jax import lax
from jax.sharding import PartitionSpec as P

NB = 512
STEPS = 2


def broadcast(value, axis, source):
    kept = jnp.where(lax.axis_index(axis) == source, value, 0).astype(value.dtype)
    return lax.psum(kept, axis)


def from_partner(block, axis, apart):
    count = lax.axis_size(axis)
    route = []
    for low in range(count):
        high = low | 1 << apart
        if high != low and high < count:
            route += [(low, high), (high, low)]
    return lax.ppermute(block, axis, route)


def global_index(count, block, grid, position):
    ladder = jnp.arange(count, dtype=jnp.int32)
    return (ladder // block * grid + position) * block + ladder % block


def times_transposed(left, right):
    return lax.dot_general(
        left,
        right,
        (((1,), (1,)), ((), ())),
        precision=lax.Precision.HIGHEST,
        preferred_element_type=jnp.float32,
    )


def local(gram):
    grid_rows = lax.axis_size("row")
    grid_cols = lax.axis_size("col")
    row_id = lax.axis_index("row")
    col_id = lax.axis_index("col")
    rblock = NB * grid_cols // grid_rows
    per_class = grid_rows // grid_cols
    local_rows = gram.shape[0]
    local_cols = gram.shape[1]
    blocks = local_rows // rblock
    grows = global_index(local_rows, rblock, grid_rows, row_id)
    gcols = global_index(local_cols, NB, grid_cols, col_id)
    member = row_id % per_class
    row_class = row_id // per_class
    identity = jnp.eye(NB, dtype=jnp.float32)

    def factor_panel(matrix, panel_index):
        owner_col = panel_index % grid_cols
        local_block = panel_index // grid_cols
        end_row = panel_index * NB + NB
        column = matrix[:, local_block * NB : (local_block + 1) * NB]
        square = column[local_block * rblock : (local_block + 1) * rblock]
        is_owner = col_id == owner_col
        in_class = row_class == owner_col
        select = (jnp.arange(per_class, dtype=jnp.int32) == member).astype(jnp.float32)
        weight = jnp.where(is_owner & in_class, 1.0, 0.0).astype(jnp.float32)
        placed = (select[:, None, None] * square[None]).reshape(NB, NB) * weight
        diagonal = lax.psum(placed, "row")
        diagonal = jnp.where(is_owner, diagonal, identity)
        low_factor = jnp.linalg.cholesky(diagonal)
        inverse = jax.scipy.linalg.solve_triangular(low_factor, identity, lower=True)
        solved = times_transposed(column, inverse)
        trailing = jnp.where((grows >= end_row)[:, None], solved, 0.0)
        rows_diag = lax.dynamic_slice_in_dim(low_factor, member * rblock, rblock, 0)
        previous = trailing[local_block * rblock : (local_block + 1) * rblock]
        patched = jnp.where(in_class, rows_diag, previous)
        factored = trailing.at[local_block * rblock : (local_block + 1) * rblock].set(patched)
        new_column = jnp.where(is_owner, factored, column)
        matrix = matrix.at[:, local_block * NB : (local_block + 1) * NB].set(new_column)
        return (matrix, trailing)

    matrix = gram
    for panel_index in range(STEPS):
        matrix, trailing = factor_panel(matrix, panel_index)
        spread_owner_col = panel_index % grid_cols
        spread_rows_all = broadcast(trailing, "col", spread_owner_col)
        pieces = spread_rows_all.reshape(grid_cols, blocks // grid_cols * rblock, NB)
        shift_bits = per_class.bit_length() - 1
        for bit_level in reversed(range(grid_cols.bit_length() - 1)):
            halfway = pieces.shape[0] // 2
            own_bit = row_class >> bit_level & 1
            wanted = col_id >> bit_level & 1
            upper = own_bit == 1
            retained = jnp.where(upper, pieces[halfway:], pieces[:halfway])
            outgoing = jnp.where(upper, pieces[:halfway], pieces[halfway:])
            received = from_partner(outgoing, "row", shift_bits + bit_level)
            pieces = jnp.where(own_bit == wanted, retained, received)
        gathered = lax.all_gather(pieces[0], "row", axis=0, tiled=True)
        spread_columns = gathered.reshape(grid_cols, per_class, blocks // grid_cols, rblock, NB)
        spread_columns = jnp.transpose(spread_columns, (0, 2, 1, 3, 4)).reshape(local_cols, NB)
        first_row = panel_index * NB
        apply_end_row = first_row + NB
        current = matrix
        updated = current - times_transposed(spread_rows_all, spread_columns)
        panel_rows = (grows >= first_row) & (grows < apply_end_row)
        beyond = gcols >= apply_end_row
        updated = jnp.where(panel_rows[:, None] & beyond[None, :], 0.0, updated)
        matrix = matrix.at[:, 0:local_cols].set(updated)
    matrix, trailing = factor_panel(matrix, STEPS)
    return matrix


def solution(mesh):
    placed = (P("row", "col"),)
    return jax.shard_map(
        local, mesh=mesh, in_specs=placed, out_specs=P("row", "col"), check_vma=False
    )
```

profile of v0, /device:TPU:0, one launch (start us, length us, event | category | flops | bytes accessed | tf_op | source)
XLA Modules:
  0.0 1543.9 jit_solution(489001765417519902)
XLA Ops:
  6.5 23.0 %copy.106 = f32[2048,4096]{1,0:T(8,128)} copy(f32[2048,4096]{1,0:T(8,128)} %param.24) | data formatting | bytes 67108864
  32.8 81.1 %all-reduce.7.cloned.1.call-done = f32[512,512]{0,1:T(8,128)} async-done(((f32[512,512]{0,1:T(8,128)}), f32[512,512]{0,1:T(8,128)}) %all-reduce.7.cloned.1.call-update) | async-done | bytes 1048592 | tf_op jit(solution)/shard_map/psum | solution.py:67
  118.1 11.7 cholesky.374
  130.0 9.8 custom-call.31
  140.5 11.7 cholesky.393
  152.3 10.0 custom-call.32
  162.9 11.7 cholesky.414
  174.6 9.8 custom-call.33
  185.1 11.7 cholesky.431
  203.0 8.4 while.16
  211.4 39.3 %custom-call.34 = f32[4,128,128]{1,2,0:T(8,128)S(1)} custom-call(f32[4,128,128]{2,1,0:T(8,128)S(1)} %get-tuple-element.139), custom_call_target="InvertDiagBlocksLowerTriangular" | custom-call | tf_op jit(solution)/shard_map/jit(_solve_triangular)/triangular_solve | solution.py:70
  255.5 10.6 broadcast_select_fusion.1
  266.2 84.3 %all-reduce.9.cloned.1.call-done = f32[2048,512]{1,0:T(8,128)} async-done(((f32[2048,512]{1,0:T(8,128)}), f32[2048,512]{1,0:T(8,128)}) %all-reduce.9.cloned.1.call-update) | async-done | bytes 4194320 | tf_op jit(solution)/shard_map/psum | solution.py:12
  350.5 4.8 slice_select_fusion.2
  357.7 90.7 %collective-permute-done = f32[2,512,512]{2,1,0:T(8,128)S(1)} collective-permute-done((f32[2,512,512]{2,1,0:T(8,128)}, f32[2,512,512]{2,1,0:T(8,128)S(1)}, u32[]{:S(2)}, u32[]{:S(2)}) %collective-permute-start) | collective-permute-done | bytes 2097184 | tf_op jit(solution)/shard_map/ppermute | solution.py:22
  453.6 23.9 %collective-permute-done.1 = f32[1,512,512]{2,1,0:T(8,128)} collective-permute-done((f32[1,512,512]{2,1,0:T(8,128)}, f32[1,512,512]{2,1,0:T(8,128)}, u32[]{:S(2)}, u32[]{:S(2)}) %collective-permute-start.1) | collective-permute-done | bytes 1048608 | tf_op jit(solution)/shard_map/ppermute | solution.py:22
  482.2 7.1 fusion
  489.3 116.8 %all-gather.5.cloned.1.call-done = f32[1,4096,512]{2,1,0:T(8,128)} async-done(((f32[1,512,512]{2,1,0:T(8,128)}), f32[1,4096,512]{2,1,0:T(8,128)}) %all-gather.5.cloned.1.call-update) | async-done | bytes 8388624 | tf_op jit(solution)/shard_map/all_gather | solution.py:97
  610.7 60.7 %subtract_select_fusion.1 = f32[2048,4096]{1,0:T(8,128)} fusion(f32[2048,4096]{1,0:T(8,128)} %fusion, pred[4096]{0:T(1024)(128)(4,1)S(1)} %broadcast_compare_fusion.1, pred[2048]{0:T(1024)(128)(4,1)S(1)} %get-tuple-element.222, f32[2048,512]{1,0:T(8,128)S(1)} %copy-done, f32[4096,512]{1,0:T(8,128)S(1)} %bitcast.177), kind=kOutput, calls=%fused_computation.7 | convolution fusion | flops 51564773376 | bytes 79697920 | tf_op jit(solution)/shard_map/dot_general | solution.py:31
  674.6 76.4 %all-reduce.11.cloned.1.call-done = f32[512,512]{0,1:T(8,128)} async-done(((f32[512,512]{0,1:T(8,128)}), f32[512,512]{0,1:T(8,128)}) %all-reduce.11.cloned.1.call-update) | async-done | bytes 1048592 | tf_op jit(solution)/shard_map/psum | solution.py:67
  754.0 11.7 cholesky.446
  765.9 9.8 custom-call.35
  776.4 11.7 cholesky.465
  788.1 10.0 custom-call.36
  798.8 11.7 cholesky.486
  810.6 9.8 custom-call.37
  821.0 11.7 cholesky.503
  839.8 8.4 while.17
  848.2 39.3 %custom-call.38 = f32[4,128,128]{1,2,0:T(8,128)S(1)} custom-call(f32[4,128,128]{2,1,0:T(8,128)S(1)} %get-tuple-element.140), custom_call_target="InvertDiagBlocksLowerTriangular" | custom-call | tf_op jit(solution)/shard_map/jit(_solve_triangular)/triangular_solve | solution.py:70
  892.3 10.6 broadcast_select_fusion
  903.1 85.0 %all-reduce.13.cloned.1.call-done = f32[2048,512]{1,0:T(8,128)} async-done(((f32[2048,512]{1,0:T(8,128)}), f32[2048,512]{1,0:T(8,128)}) %all-reduce.13.cloned.1.call-update) | async-done | bytes 4194320 | tf_op jit(solution)/shard_map/psum | solution.py:12
  993.4 90.5 %collective-permute-done.2 = f32[2,512,512]{2,1,0:T(8,128)S(1)} collective-permute-done((f32[2,512,512]{2,1,0:T(8,128)S(1)}, f32[2,512,512]{2,1,0:T(8,128)S(1)}, u32[]{:S(2)}, u32[]{:S(2)}) %collective-permute-start.2) | collective-permute-done | bytes 2097184 | tf_op jit(solution)/shard_map/ppermute | solution.py:22
  1085.1 23.7 %collective-permute-done.3 = f32[1,512,512]{2,1,0:T(8,128)S(1)} collective-permute-done((f32[1,512,512]{2,1,0:T(8,128)S(1)}, f32[1,512,512]{2,1,0:T(8,128)S(1)}, u32[]{:S(2)}, u32[]{:S(2)}) %collective-permute-start.3) | collective-permute-done | bytes 1048608 | tf_op jit(solution)/shard_map/ppermute | solution.py:22
  1112.3 5.8 fusion.1
  1118.1 118.1 %all-gather.7.cloned.1.call-done = f32[1,4096,512]{2,1,0:T(8,128)} async-done(((f32[1,512,512]{2,1,0:T(8,128)}), f32[1,4096,512]{2,1,0:T(8,128)}) %all-gather.7.cloned.1.call-update) | async-done | bytes 8388624 | tf_op jit(solution)/shard_map/all_gather | solution.py:97
  1240.8 60.9 %subtract_select_fusion = f32[2048,4096]{1,0:T(8,128)} fusion(f32[2048,4096]{1,0:T(8,128)} %fusion.1, pred[4096]{0:T(1024)(128)(4,1)S(1)} %broadcast_compare_fusion, pred[2048]{0:T(1024)(128)(4,1)S(1)} %compare_and_fusion.1, f32[2048,512]{1,0:T(8,128)S(1)} %copy-done.1, f32[4096,512]{1,0:T(8,128)S(1)} %bitcast.178), kind=kOutput, calls=%fused_computation.6 | convolution fusion | flops 51564773376 | bytes 79697920 | tf_op jit(solution)/shard_map/dot_general | solution.py:31
  1304.6 76.6 %all-reduce.15.cloned.1.call-done = f32[512,512]{0,1:T(8,128)} async-done(((f32[512,512]{0,1:T(8,128)}), f32[512,512]{0,1:T(8,128)}) %all-reduce.15.cloned.1.call-update) | async-done | bytes 1048592 | tf_op jit(solution)/shard_map/psum | solution.py:67
  1384.3 11.7 cholesky.518
  1396.1 9.8 custom-call.39
  1406.6 11.7 cholesky.537
  1418.4 10.2 custom-call.40
  1429.3 11.7 cholesky.558
  1441.0 9.8 custom-call.41
  1451.4 11.9 cholesky.575
  1469.8 8.1 while.18
  1478.0 39.3 %custom-call.42 = f32[4,128,128]{1,2,0:T(8,128)S(1)} custom-call(f32[4,128,128]{2,1,0:T(8,128)S(1)} %get-tuple-element.141), custom_call_target="InvertDiagBlocksLowerTriangular" | custom-call | tf_op jit(solution)/shard_map/jit(_solve_triangular)/triangular_solve | solution.py:70
  1522.1 8.7 fusion.14
  1531.0 5.8 fusion.2
  (199 shorter events, 108.4 us)
Async XLA Ops:
  6.5 107.3 %all-reduce.7.cloned.1.call-start = ((), (), s32[]{:S(2)}) async-start(), calls=%async_computation | async-start | bytes 2097152 | tf_op jit(solution)/shard_map/psum | solution.py:67
  32.6 317.9 %all-reduce.9.cloned.1.call-start = ((), (), s32[]{:S(2)}) async-start(), calls=%async_computation.1 | async-start | bytes 8388608 | tf_op jit(solution)/shard_map/psum | solution.py:12
  113.9 2.8 copy-start.2
  266.2 340.0 %all-gather.5.cloned.1.call-start = ((), (), s32[]{:S(2)}) async-start(), calls=%async_computation.5 | async-start | bytes 9437184 | tf_op jit(solution)/shard_map/all_gather | solution.py:97
  355.3 93.1 %collective-permute-start = (f32[2,512,512]{2,1,0:T(8,128)}, f32[2,512,512]{2,1,0:T(8,128)S(1)}, u32[]{:S(2)}, u32[]{:S(2)}) collective-permute-start(f32[2,512,512]{2,1,0:T(8,128)} %bitcast.13), channel_id=1, source_target_pairs={{0,16},{16,0},{4,20},{20,4},{8,24},{24,8},{12,28},{28,12},{1,17},{... | collective-permute-start | bytes 6291464 | tf_op jit(solution)/shard_map/ppermute | solution.py:22
  448.4 1.3 copy-start.7
  453.0 24.5 %collective-permute-start.1 = (f32[1,512,512]{2,1,0:T(8,128)}, f32[1,512,512]{2,1,0:T(8,128)}, u32[]{:S(2)}, u32[]{:S(2)}) collective-permute-start(f32[1,512,512]{2,1,0:T(8,128)} %slice_select_fusion.5), channel_id=1, source_target_pairs={{0,8},{8,0},{4,12},{12,4},{16,24},{24,16},{20,28},{28,20},{1,9},{9... | collective-permute-start | bytes 3145736 | tf_op jit(solution)/shard_map/ppermute | solution.py:22
  478.9 272.1 %all-reduce.11.cloned.1.call-start = ((), (), s32[]{:S(2)}) async-start(), calls=%async_computation.2 | async-start | bytes 2097152 | tf_op jit(solution)/shard_map/psum | solution.py:67
  606.1 4.6 copy-start
  674.4 313.7 %all-reduce.13.cloned.1.call-start = ((), (), s32[]{:S(2)}) async-start(), calls=%async_computation.3 | async-start | bytes 8388608 | tf_op jit(solution)/shard_map/psum | solution.py:12
  751.0 1.5 copy-start.3
  902.9 333.3 %all-gather.7.cloned.1.call-start = ((), (), s32[]{:S(2)}) async-start(), calls=%async_computation.6 | async-start | bytes 9437184 | tf_op jit(solution)/shard_map/all_gather | solution.py:97
  990.9 93.0 %collective-permute-start.2 = (f32[2,512,512]{2,1,0:T(8,128)S(1)}, f32[2,512,512]{2,1,0:T(8,128)S(1)}, u32[]{:S(2)}, u32[]{:S(2)}) collective-permute-start(f32[2,512,512]{2,1,0:T(8,128)S(1)} %bitcast.189), channel_id=1, source_target_pairs={{0,16},{16,0},{4,20},{20,4},{8,24},{24,8},{12,28},{28,12},{1,17},{... | collective-permute-start | bytes 6291464 | tf_op jit(solution)/shard_map/ppermute | solution.py:22
  1084.3 26.0 %copy-start.5 = (f32[512,512]{1,0:T(8,128)S(1)}, f32[512,512]{1,0:T(8,128)}, u32[]{:S(2)}) copy-start(f32[512,512]{1,0:T(8,128)} %get-tuple-element.169) | copy-start | bytes 3145732
  1084.6 24.2 %collective-permute-start.3 = (f32[1,512,512]{2,1,0:T(8,128)S(1)}, f32[1,512,512]{2,1,0:T(8,128)S(1)}, u32[]{:S(2)}, u32[]{:S(2)}) collective-permute-start(f32[1,512,512]{2,1,0:T(8,128)S(1)} %slice_select_fusion.4), channel_id=1, source_target_pairs={{0,8},{8,0},{4,12},{12,4},{16,24},{24,16},{20,28},{28,20},{1,9},{9... | collective-permute-start | bytes 3145736 | tf_op jit(solution)/shard_map/ppermute | solution.py:22
  1110.2 271.1 %all-reduce.15.cloned.1.call-start = ((), (), s32[]{:S(2)}) async-start(), calls=%async_computation.4 | async-start | bytes 2097152 | tf_op jit(solution)/shard_map/psum | solution.py:67
  1236.2 4.6 copy-start.1
  1381.3 1.5 copy-start.4
  1522.1 8.7 copy-start.6
Sparse Core Ops, SparseCore 0:
  32.7 81.0 all-reduce.6
  266.3 84.1 all-reduce.8
  479.1 127.0 all-gather.4
  674.5 76.4 all-reduce.10
  903.0 85.0 all-reduce.12
  1110.3 125.8 all-gather.6
  1304.7 76.4 all-reduce.14
where the time goes:
time: 1550 us; the launch traced here: 1540 us
  waiting for transfers between devices  867 us (56%)
  other arithmetic  408 us (26%)
  matrix products  171 us (11%)
  local copies, waits for them, and re-layouts  67.9 us (4%)
  between operations  22.3 us (1%)
    another operation x44, other arithmetic, factor_panel(): low_factor = jnp.linalg.cholesky(diagonal)  238 us
    all_gather x2, waiting for transfers between devices, local(): gathered = lax.all_gather(pieces[0], 'row', axis=0, tiled=True)  235 us
    psum x3, waiting for transfers between devices, factor_panel(): diagonal = lax.psum(placed, 'row')  234 us
    ppermute x4, waiting for transfers between devices, from_partner(): return lax.ppermute(block, axis, route)  229 us
    psum x2, waiting for transfers between devices, broadcast(): return lax.psum(kept, axis)  169 us
    dot_general x5, matrix products, times_transposed(): lax.dot_general(left, right, (((1,), (1,)), ((), ())), precision=lax.Prec...  152 us
    another operation x7, other arithmetic, factor_panel(): jax.scipy.linalg.solve_triangular(low_factor, identity, lower=True)  122 us
  transfers between devices with their start and end apart: 11, of which 11 were waited for; matrix products, arithmetic and copies ran while one was open for 1% of the time, Pallas kernels for 0%

commit v1 on v0

--- a/solution.py
+++ b/solution.py
@@ -9,7 +9,7 @@
 
 def broadcast(value, axis, source):
     kept = jnp.where(lax.axis_index(axis) == source, value, 0).astype(value.dtype)
-    return lax.psum(kept, axis)
+    return jnp.sum(lax.all_gather(kept, axis), axis=0)
 
 
 def from_partner(block, axis, apart):

time: 1550 us -> 1630 us (1.052)
  waiting for transfers between devices: 867 us -> 909 us
  other arithmetic: 408 us -> 439 us
    all_gather x0 -> x2, waiting for transfers between devices: none -> 210 us  [broadcast(): return jnp.sum(lax.all_gather(kept, axis), axis=0)]
    psum x2 -> x0, waiting for transfers between devices: 169 us -> none  [broadcast(): return lax.psum(kept, axis)]
    reduce_sum x0 -> x2, other arithmetic: none -> 20.6 us  [broadcast(): return jnp.sum(lax.all_gather(kept, axis), axis=0)]
where the time goes in v1:
time: 1630 us; the launch traced here: 1620 us
  waiting for transfers between devices  909 us (56%)
  other arithmetic  439 us (27%)
  matrix products  171 us (10%)
  local copies, waits for them, and re-layouts  67.5 us (4%)
  between operations  22.3 us (1%)
    another operation x44, other arithmetic, factor_panel(): low_factor = jnp.linalg.cholesky(diagonal)  248 us
    psum x3, waiting for transfers between devices, factor_panel(): diagonal = lax.psum(placed, 'row')  234 us
    all_gather x2, waiting for transfers between devices, local(): gathered = lax.all_gather(pieces[0], 'row', axis=0, tiled=True)  233 us
    ppermute x4, waiting for transfers between devices, from_partner(): return lax.ppermute(block, axis, route)  231 us
    all_gather x2, waiting for transfers between devices, broadcast(): return jnp.sum(lax.all_gather(kept, axis), axis=0)  210 us
    dot_general x5, matrix products, times_transposed(): lax.dot_general(left, right, (((1,), (1,)), ((), ())), precision=lax.Prec...  152 us
    another operation x7, other arithmetic, factor_panel(): jax.scipy.linalg.solve_triangular(low_factor, identity, lower=True)  122 us
  transfers between devices with their start and end apart: 11, of which 11 were waited for; matrix products, arithmetic and copies ran while one was open for 1% of the time, Pallas kernels for 0%

profile of v1, /device:TPU:0, one launch (start us, length us, event | category | flops | bytes accessed | tf_op | source)
XLA Modules:
  0.0 1615.8 jit_solution(1784925896366007515)
XLA Ops:
  6.5 23.0 %copy.106 = f32[2048,4096]{1,0:T(8,128)} copy(f32[2048,4096]{1,0:T(8,128)} %param.24) | data formatting | bytes 67108864
  32.8 81.1 %all-reduce.5.cloned.1.call-done = f32[512,512]{0,1:T(8,128)} async-done(((f32[512,512]{0,1:T(8,128)}), f32[512,512]{0,1:T(8,128)}) %all-reduce.5.cloned.1.call-update) | async-done | bytes 1048592 | tf_op jit(solution)/shard_map/psum | solution.py:67
  118.1 11.7 cholesky.374
  130.0 9.8 custom-call.31
  140.5 11.7 cholesky.393
  152.3 10.0 custom-call.32
  163.0 11.7 cholesky.414
  174.7 9.8 custom-call.33
  185.1 11.7 cholesky.431
  196.9 11.2 compare_reduce_fusion.9
  213.3 8.1 while.16
  221.5 39.3 %custom-call.34 = f32[4,128,128]{1,2,0:T(8,128)S(1)} custom-call(f32[4,128,128]{2,1,0:T(8,128)S(1)} %get-tuple-element.139), custom_call_target="InvertDiagBlocksLowerTriangular" | custom-call | tf_op jit(solution)/shard_map/jit(_solve_triangular)/triangular_solve | solution.py:70
  265.6 10.5 broadcast_select_fusion.1
  276.2 104.7 %all-gather.9.cloned.1.call-done = f32[8192,512]{1,0:T(8,128)} async-done(((f32[2048,512]{1,0:T(8,128)}), f32[8192,512]{1,0:T(8,128)}) %all-gather.9.cloned.1.call-update) | async-done | bytes 16777232 | tf_op jit(solution)/shard_map/all_gather | solution.py:12
  380.9 10.3 reduce_sum.18
  398.4 91.4 %collective-permute-done = f32[2,512,512]{2,1,0:T(8,128)S(1)} collective-permute-done((f32[2,512,512]{2,1,0:T(8,128)}, f32[2,512,512]{2,1,0:T(8,128)S(1)}, u32[]{:S(2)}, u32[]{:S(2)}) %collective-permute-start) | collective-permute-done | bytes 2097184 | tf_op jit(solution)/shard_map/ppermute | solution.py:22
  495.0 24.2 %collective-permute-done.1 = f32[1,512,512]{2,1,0:T(8,128)} collective-permute-done((f32[1,512,512]{2,1,0:T(8,128)}, f32[1,512,512]{2,1,0:T(8,128)}, u32[]{:S(2)}, u32[]{:S(2)}) %collective-permute-start.1) | collective-permute-done | bytes 1048608 | tf_op jit(solution)/shard_map/ppermute | solution.py:22
  523.9 7.2 fusion
  531.1 116.0 %all-gather.11.cloned.1.call-done = f32[1,4096,512]{2,1,0:T(8,128)} async-done(((f32[1,512,512]{2,1,0:T(8,128)}), f32[1,4096,512]{2,1,0:T(8,128)}) %all-gather.11.cloned.1.call-update) | async-done | bytes 8388624 | tf_op jit(solution)/shard_map/all_gather | solution.py:97
  651.7 60.7 %subtract_select_fusion.1 = f32[2048,4096]{1,0:T(8,128)} fusion(f32[2048,4096]{1,0:T(8,128)} %fusion, pred[4096]{0:T(1024)(128)(4,1)S(1)} %broadcast_compare_fusion.1, pred[2048]{0:T(1024)(128)(4,1)S(1)} %compare_and_fusion, f32[2048,512]{1,0:T(8,128)S(1)} %copy-done, f32[4096,512]{1,0:T(8,128)S(1)} %bitcast.179), kind=kOutput, calls=%fused_computation.7 | convolution fusion | flops 51564773376 | bytes 79697920 | tf_op jit(solution)/shard_map/dot_general | solution.py:31
  715.6 76.4 %all-reduce.7.cloned.1.call-done = f32[512,512]{0,1:T(8,128)} async-done(((f32[512,512]{0,1:T(8,128)}), f32[512,512]{0,1:T(8,128)}) %all-reduce.7.cloned.1.call-update) | async-done | bytes 1048592 | tf_op jit(solution)/shard_map/psum | solution.py:67
  795.0 11.7 cholesky.446
  806.9 9.8 custom-call.35
  817.4 11.7 cholesky.465
  829.2 10.0 custom-call.36
  839.8 11.7 cholesky.486
  851.6 9.8 custom-call.37
  862.0 11.7 cholesky.503
  880.8 8.1 while.17
  888.9 39.3 %custom-call.38 = f32[4,128,128]{1,2,0:T(8,128)S(1)} custom-call(f32[4,128,128]{2,1,0:T(8,128)S(1)} %get-tuple-element.140), custom_call_target="InvertDiagBlocksLowerTriangular" | custom-call | tf_op jit(solution)/shard_map/jit(_solve_triangular)/triangular_solve | solution.py:70
  933.0 10.5 broadcast_select_fusion
  943.8 105.4 %all-gather.13.cloned.1.call-done = f32[8192,512]{1,0:T(8,128)} async-done(((f32[2048,512]{1,0:T(8,128)}), f32[8192,512]{1,0:T(8,128)}) %all-gather.13.cloned.1.call-update) | async-done | bytes 16777232 | tf_op jit(solution)/shard_map/all_gather | solution.py:12
  1049.2 10.3 reduce_sum.19
  1064.8 91.2 %collective-permute-done.2 = f32[2,512,512]{2,1,0:T(8,128)S(1)} collective-permute-done((f32[2,512,512]{2,1,0:T(8,128)S(1)}, f32[2,512,512]{2,1,0:T(8,128)S(1)}, u32[]{:S(2)}, u32[]{:S(2)}) %collective-permute-start.2) | collective-permute-done | bytes 2097184 | tf_op jit(solution)/shard_map/ppermute | solution.py:22
  1157.3 24.0 %collective-permute-done.3 = f32[1,512,512]{2,1,0:T(8,128)S(1)} collective-permute-done((f32[1,512,512]{2,1,0:T(8,128)S(1)}, f32[1,512,512]{2,1,0:T(8,128)S(1)}, u32[]{:S(2)}, u32[]{:S(2)}) %collective-permute-start.3) | collective-permute-done | bytes 1048608 | tf_op jit(solution)/shard_map/ppermute | solution.py:22
  1190.6 117.4 %all-gather.15.cloned.1.call-done = f32[1,4096,512]{2,1,0:T(8,128)} async-done(((f32[1,512,512]{2,1,0:T(8,128)}), f32[1,4096,512]{2,1,0:T(8,128)}) %all-gather.15.cloned.1.call-update) | async-done | bytes 8388624 | tf_op jit(solution)/shard_map/all_gather | solution.py:97
  1312.5 61.1 %subtract_select_fusion = f32[2048,4096]{1,0:T(8,128)} fusion(f32[2048,4096]{1,0:T(8,128)} %fusion.1, pred[4096]{0:T(1024)(128)(4,1)S(1)} %broadcast_compare_fusion, pred[2048]{0:T(1024)(128)(4,1)S(1)} %compare_and_fusion.1, f32[2048,512]{1,0:T(8,128)S(1)} %copy-done.1, f32[4096,512]{1,0:T(8,128)S(1)} %bitcast.180), kind=kOutput, calls=%fused_computation.6 | convolution fusion | flops 51564773376 | bytes 79697920 | tf_op jit(solution)/shard_map/dot_general | solution.py:31
  1376.6 76.6 %all-reduce.9.cloned.1.call-done = f32[512,512]{0,1:T(8,128)} async-done(((f32[512,512]{0,1:T(8,128)}), f32[512,512]{0,1:T(8,128)}) %all-reduce.9.cloned.1.call-update) | async-done | bytes 1048592 | tf_op jit(solution)/shard_map/psum | solution.py:67
  1456.2 11.7 cholesky.518
  1468.1 9.8 custom-call.39
  1478.6 11.7 cholesky.537
  1490.3 10.0 custom-call.40
  1501.0 11.7 cholesky.558
  1512.7 9.8 custom-call.41
  1523.1 11.9 cholesky.575
  1541.6 8.1 while.18
  1549.7 39.3 %custom-call.42 = f32[4,128,128]{1,2,0:T(8,128)S(1)} custom-call(f32[4,128,128]{2,1,0:T(8,128)S(1)} %get-tuple-element.141), custom_call_target="InvertDiagBlocksLowerTriangular" | custom-call | tf_op jit(solution)/shard_map/jit(_solve_triangular)/triangular_solve | solution.py:70
  1593.9 8.7 fusion.14
  (201 shorter events, 123.7 us)
Async XLA Ops:
  6.5 107.3 %all-reduce.5.cloned.1.call-start = ((), (), s32[]{:S(2)}) async-start(), calls=%async_computation | async-start | bytes 2097152 | tf_op jit(solution)/shard_map/psum | solution.py:67
  32.6 348.3 %all-gather.9.cloned.1.call-start = ((), (), s32[]{:S(2)}) async-start(), calls=%async_computation.3 | async-start | bytes 20971520 | tf_op jit(solution)/shard_map/all_gather | solution.py:12
  113.9 2.8 copy-start.2
  276.2 371.0 %all-gather.11.cloned.1.call-start = ((), (), s32[]{:S(2)}) async-start(), calls=%async_computation.4 | async-start | bytes 9437184 | tf_op jit(solution)/shard_map/all_gather | solution.py:97
  396.0 93.8 %collective-permute-start = (f32[2,512,512]{2,1,0:T(8,128)}, f32[2,512,512]{2,1,0:T(8,128)S(1)}, u32[]{:S(2)}, u32[]{:S(2)}) collective-permute-start(f32[2,512,512]{2,1,0:T(8,128)} %bitcast.14), channel_id=1, source_target_pairs={{0,16},{16,0},{4,20},{20,4},{8,24},{24,8},{12,28},{28,12},{1,17},{... | collective-permute-start | bytes 6291464 | tf_op jit(solution)/shard_map/ppermute | solution.py:22
  489.9 1.3 copy-start.7
  494.4 24.8 %collective-permute-start.1 = (f32[1,512,512]{2,1,0:T(8,128)}, f32[1,512,512]{2,1,0:T(8,128)}, u32[]{:S(2)}, u32[]{:S(2)}) collective-permute-start(f32[1,512,512]{2,1,0:T(8,128)} %slice_select_fusion.5), channel_id=1, source_target_pairs={{0,8},{8,0},{4,12},{12,4},{16,24},{24,16},{20,28},{28,20},{1,9},{9... | collective-permute-start | bytes 3145736 | tf_op jit(solution)/shard_map/ppermute | solution.py:22
  520.6 271.4 %all-reduce.7.cloned.1.call-start = ((), (), s32[]{:S(2)}) async-start(), calls=%async_computation.1 | async-start | bytes 2097152 | tf_op jit(solution)/shard_map/psum | solution.py:67
  647.1 4.6 copy-start
  715.4 333.8 %all-gather.13.cloned.1.call-start = ((), (), s32[]{:S(2)}) async-start(), calls=%async_computation.5 | async-start | bytes 20971520 | tf_op jit(solution)/shard_map/all_gather | solution.py:12
  792.1 1.5 copy-start.3
  943.5 364.4 %all-gather.15.cloned.1.call-start = ((), (), s32[]{:S(2)}) async-start(), calls=%async_computation.6 | async-start | bytes 9437184 | tf_op jit(solution)/shard_map/all_gather | solution.py:97
  1062.3 93.7 %collective-permute-start.2 = (f32[2,512,512]{2,1,0:T(8,128)S(1)}, f32[2,512,512]{2,1,0:T(8,128)S(1)}, u32[]{:S(2)}, u32[]{:S(2)}) collective-permute-start(f32[2,512,512]{2,1,0:T(8,128)S(1)} %bitcast.193), channel_id=1, source_target_pairs={{0,16},{16,0},{4,20},{20,4},{8,24},{24,8},{12,28},{28,12},{1,17},{... | collective-permute-start | bytes 6291464 | tf_op jit(solution)/shard_map/ppermute | solution.py:22
  1156.5 26.3 %copy-start.5 = (f32[512,512]{1,0:T(8,128)S(1)}, f32[512,512]{1,0:T(8,128)}, u32[]{:S(2)}) copy-start(f32[512,512]{1,0:T(8,128)} %get-tuple-element.169) | copy-start | bytes 3145732
  1156.7 24.5 %collective-permute-start.3 = (f32[1,512,512]{2,1,0:T(8,128)S(1)}, f32[1,512,512]{2,1,0:T(8,128)S(1)}, u32[]{:S(2)}, u32[]{:S(2)}) collective-permute-start(f32[1,512,512]{2,1,0:T(8,128)S(1)} %slice_select_fusion.4), channel_id=1, source_target_pairs={{0,8},{8,0},{4,12},{12,4},{16,24},{24,16},{20,28},{28,20},{1,9},{9... | collective-permute-start | bytes 3145736 | tf_op jit(solution)/shard_map/ppermute | solution.py:22
  1182.7 270.6 %all-reduce.9.cloned.1.call-start = ((), (), s32[]{:S(2)}) async-start(), calls=%async_computation.2 | async-start | bytes 2097152 | tf_op jit(solution)/shard_map/psum | solution.py:67
  1307.9 4.6 copy-start.1
  1453.2 1.5 copy-start.4
  1593.8 8.7 copy-start.6
Sparse Core Ops, SparseCore 0:
  32.7 81.0 all-reduce.4
  276.3 104.5 all-gather.8
  520.8 126.3 all-gather.10
  715.5 76.5 all-reduce.6
  943.7 105.4 all-gather.12
  1182.8 125.1 all-gather.14
  1376.7 76.4 all-reduce.8
